TPU v7x, 512 devices: a whole 4x8x8 slice. The times are simulated.
512 devices in a mesh: dp: 64 (over z, y_hi, core), seq: 8 (over y_lo, x).
Axes of the slice: x: 4, y: 8 (y_hi: 4, y_lo: 2; y = y_hi * 2 + y_lo), z: 8, core: 2. Of those that a mesh axis runs over, the one named last changes fastest.
Arguments:
- tokens: bfloat16 [1024, 4096], P('seq', 'dp'), may hold values from -6 to 6
- in_weight: bfloat16 [2, 4096, 8192], P(None, 'seq', 'dp'), may hold values from -0.09375 to 0.09375
- conv_weight: bfloat16 [4, 8192], P(None, 'dp'), may hold values from -0.5 to 0.5
- conv_bias: bfloat16 [8192], P('dp'), may hold values from -1 to 1
- out_weight: bfloat16 [8192, 4096], P('dp', 'seq'), may hold values from -0.0625 to 0.0625
- grad_out: bfloat16 [1024, 4096], P('seq', 'dp'), may hold values from -6 to 6
Outputs:
- output: bfloat16 [1024, 4096], P('seq', 'dp')
- grad_tokens: bfloat16 [1024, 4096], P('seq', 'dp')
- grad_in_weight: float32 [2, 4096, 8192], P(None, 'seq', 'dp')
- grad_out_weight: float32 [8192, 4096], P('dp', 'seq')
- grad_conv_weight: float32 [4, 8192], P(None, 'dp')
- grad_conv_bias: float32 [8192], P('dp')
All inputs are finite; a program needn't handle non-finite values.
Results may differ from a plain program's by a relative error of at most 0.012.
Values may be sent and summed in bfloat16 or wider, within the bound.
No kernel may reach another device: no remote copies, remote signals or barrier semaphores. Data moves between devices by JAX's collectives and lax.ppermute only.
A program may use at most 64 MiB of HBM per device.

v0:
```python
import jax
import jax.numpy as jnp
from jax import lax
from jax.sharding import PartitionSpec as P

DP = ("chip", "core")


def from_behind(block, axis, distance):
    devices = range(lax.axis_size(axis))
    route = [(i - distance, i) for i in devices if i - distance in devices]
    return lax.ppermute(block, axis, route)


def silu_parts(value):
    sig = jax.nn.sigmoid(value)
    return (value * sig, sig * (1.0 + value * (1.0 - sig)))


def gather_over(block, axis, n, dim):
    rep = jnp.broadcast_to(block[None], (n,) + block.shape)
    return lax.all_to_all(rep, axis, 0, dim + 1, tiled=True)[0]


def split_exact(value):
    hi = value.astype(jnp.bfloat16)
    rest = value - hi.astype(jnp.float32)
    mid = rest.astype(jnp.bfloat16)
    lo = (rest - mid.astype(jnp.float32)).astype(jnp.bfloat16)
    return jnp.concatenate([hi, mid, lo], axis=0)


def reduce_over_dp(part, n_chip, n_core):
    split = part.astype(jnp.bfloat16)
    split = split.reshape((n_chip, n_core, part.shape[0] // (n_chip * n_core)) + part.shape[1:])
    split = lax.all_to_all(split, "core", 1, 1, tiled=True).astype(jnp.float32).sum(axis=1)
    split = split.astype(jnp.bfloat16)
    return lax.all_to_all(split, "chip", 0, 0, tiled=True).astype(jnp.float32).sum(axis=0)


def on_device(tokens, in_weight, conv_weight, conv_bias, out_weight, grad_out):
    n_seq = lax.axis_size("seq")
    n_chip = lax.axis_size("chip")
    n_core = lax.axis_size("core")
    n_dp = n_chip * n_core
    w_local = jnp.concatenate([in_weight, out_weight.T[None]], axis=0)
    w_full = lax.all_gather(w_local, "seq", axis=1, tiled=True)
    in_full = w_full[:2]
    out_full_t = w_full[2]
    acts = gather_over(jnp.stack([tokens, grad_out], axis=1), "chip", n_chip, 2)
    acts = gather_over(acts.reshape(acts.shape[:2] + (n_chip, 1, -1)), "core", n_core, 3)
    acts = acts.reshape(acts.shape[:2] + (-1,))
    whole = acts[:, 0]
    upstream = acts[:, 1]
    tok_rows = whole.shape[0]
    taps = conv_weight.shape[0]
    mixed = jnp.einsum("td,pde->tpe", whole, in_full, preferred_element_type=jnp.float32).astype(
        jnp.bfloat16
    )
    inner = mixed[:, 0, :]
    gate_in = mixed[:, 1, :]
    rim = from_behind(inner[tok_rows - (taps - 1) :], "seq", 1)
    padded = jnp.concatenate([rim, inner], axis=0)
    conv = jnp.broadcast_to(conv_bias.astype(jnp.float32)[None, :], inner.shape)
    for lag in range(taps):
        conv = conv + conv_weight[lag].astype(jnp.float32)[None, :] * padded[
            lag : lag + tok_rows
        ].astype(jnp.float32)
    act, act_slope = silu_parts(conv)
    gate, gate_slope = silu_parts(gate_in.astype(jnp.float32))
    hidden = (act * gate).astype(jnp.bfloat16)
    out_part = jnp.einsum("te,de->dt", hidden, out_full_t, preferred_element_type=jnp.float32)
    back = jnp.einsum("td,de->te", upstream, out_full_t, preferred_element_type=jnp.float32)
    grad_conv = (back * gate * act_slope).astype(jnp.bfloat16)
    grad_gate = (back * act * gate_slope).astype(jnp.bfloat16)
    ahead_rim = from_behind(grad_conv[: taps - 1], "seq", -1)
    ahead = jnp.concatenate([grad_conv, ahead_rim], axis=0)
    grad_inner = jnp.zeros(inner.shape, jnp.float32)
    for lag in range(taps):
        shift_start = taps - 1 - lag
        grad_inner = grad_inner + conv_weight[lag].astype(jnp.float32)[None, :] * ahead[
            shift_start : shift_start + tok_rows
        ].astype(jnp.float32)
    grad_inner = grad_inner.astype(jnp.bfloat16)
    conv_float = grad_conv.astype(jnp.float32)
    tap_rows = []
    for lag in range(taps):
        tap_rows.append(
            jnp.sum(conv_float * padded[lag : lag + tok_rows].astype(jnp.float32), axis=0)
        )
    conv_grads = jnp.concatenate(
        [jnp.stack(tap_rows, axis=0), jnp.sum(conv_float, axis=0)[None]], axis=0
    )
    branch_grads = jnp.stack([grad_inner, grad_gate], axis=1)
    tok_part = jnp.einsum("tpe,pde->dt", branch_grads, in_full, preferred_element_type=jnp.float32)
    reduced = reduce_over_dp(jnp.stack([out_part, tok_part], axis=1), n_chip, n_core)
    output = reduced[:, 0].T.astype(jnp.bfloat16)
    grad_tokens = reduced[:, 1].T.astype(jnp.bfloat16)
    term_in = jnp.einsum("td,tpe->pde", whole, branch_grads, preferred_element_type=jnp.float32)
    term_out_t = jnp.einsum("td,te->de", upstream, hidden, preferred_element_type=jnp.float32)
    terms = jnp.concatenate([term_in, term_out_t[None]], axis=0).astype(jnp.bfloat16)
    terms = lax.psum_scatter(terms, "seq", scatter_dimension=1, tiled=True).astype(jnp.float32)
    grad_in_weight = terms[:2]
    grad_out_weight = terms[2].T
    conv_parts = split_exact(conv_grads)
    conv_parts = jnp.broadcast_to(conv_parts[None], (n_seq,) + conv_parts.shape)
    parts = lax.all_to_all(conv_parts, "seq", 0, 0, tiled=True).astype(jnp.float32).sum(axis=0)
    n_row = taps + 1
    conv_grads = parts[:n_row] + parts[n_row : 2 * n_row] + parts[2 * n_row :]
    tap_grads = conv_grads[:taps]
    bias_grads = conv_grads[taps]
    return (output, grad_tokens, grad_in_weight, grad_out_weight, tap_grads, bias_grads)


def solution(mesh):
    n_core = 2
    devices = mesh.devices.reshape(mesh.devices.shape[0] // n_core, n_core, mesh.devices.shape[1])
    split_mesh = jax.sharding.Mesh(devices, ("chip", "core", "seq"))
    return jax.shard_map(
        on_device,
        mesh=split_mesh,
        in_specs=(P("seq", DP), P(None, "seq", DP), P(None, DP), P(DP), P(DP, "seq"), P("seq", DP)),
        out_specs=(
            P("seq", DP),
            P("seq", DP),
            P(None, "seq", DP),
            P(DP, "seq"),
            P(None, DP),
            P(DP),
        ),
        check_vma=False,
    )
```

profile of v0, /device:TPU:16, one launch (start us, length us, event | category | flops | bytes accessed | tf_op | source)
XLA Modules:
  0.0 184.7 jit_solution(6815564811677252783)
XLA Ops:
  7.2 1.0 copy.62
  8.3 1.7 pad_maximum_fusion.2
  10.0 0.7 pad_maximum_fusion.8
  10.8 1.2 broadcast_in_dim.19
  12.0 16.1 %all-to-all-start = ((bf16[32,128,2,64]{1,3,2,0:T(8,128)(2,1)}), bf16[32,128,2,64]{1,3,2,0:T(8,128)(2,1)S(1)}, u32[]{:S(2)}, u32[]{:S(2)}) async-start(bf16[32,128,2,64]{1,3,2,0:T(8,128)(2,1)} %broadcast_in_dim.19), calls=%async_computation | async-start | bytes 2097152 | tf_op jit(solution)/shard_map/all_to_all | solution.py:22
  28.2 37.0 %all-to-all-done = bf16[32,128,2,64]{1,3,2,0:T(8,128)(2,1)S(1)} async-done(((bf16[32,128,2,64]{1,3,2,0:T(8,128)(2,1)}), bf16[32,128,2,64]{1,3,2,0:T(8,128)(2,1)S(1)}, u32[]{:S(2)}, u32[]{:S(2)}) %all-to-all-start) | async-done | bytes 1048608 | tf_op jit(solution)/shard_map/all_to_all | solution.py:22
  65.2 0.6 broadcast_in_dim.21
  65.9 5.4 %all_to_all.45 = bf16[2,128,2,32,1,64]{1,5,3,2,4,0:T(8,128)(2,1)S(1)} all-to-all(bf16[2,128,2,32,1,64]{1,5,3,2,4,0:T(8,128)(2,1)S(1)} %broadcast_in_dim.21), channel_id=1, replica_groups=mesh['chip'=32,'core'=2,'seq'=8] {'core'}, dimensions={0} | all-to-all | bytes 4194304 | tf_op jit(solution)/shard_map/all_to_all | solution.py:22
  71.5 12.4 %all-gather.2.cloned.1.call-done = bf16[3,4096,128]{2,1,0:T(8,128)(2,1)} async-done(((bf16[3,512,128]{2,1,0:T(8,128)(2,1)}), bf16[3,4096,128]{2,1,0:T(8,128)(2,1)}) %all-gather.2.cloned.1.call-update) | async-done | bytes 3145744 | tf_op jit(solution)/shard_map/all_gather | solution.py:47
  83.8 2.3 %fusion.6 = bf16[128,2,128]{2,0,1:T(8,128)(2,1)S(1)} fusion(bf16[3,4096,128]{2,1,0:T(8,128)(2,1)} %all-gather.2.cloned.1.call-done, bf16[128,2,4096]{0,2,1:T(8,128)(2,1)S(1)} %bitcast.110), kind=kOutput, calls=%fused_computation.12 | convolution fusion | flops 268468224 | bytes 3211264 | tf_op jit(solution)/shard_map/td,pde->tpe/dot_general | solution.py:57
  86.2 2.4 %collective-permute-start = (bf16[3,128]{1,0:T(4,128)(2,1)S(1)}, bf16[3,128]{1,0:T(4,128)(2,1)S(1)}, u32[]{:S(2)}, u32[]{:S(2)}) collective-permute-start(bf16[3,128]{1,0:T(4,128)(2,1)S(1)} %slice_bitcast_fusion.11), channel_id=1, source_target_pairs={{0,1},{1,2},{2,3},{3,4},{4,5},{5,6},{6,7},{8,9},{9,10},{10,11},{11... | collective-permute-start | bytes 2312 | tf_op jit(solution)/shard_map/ppermute | solution.py:12
  88.5 1.3 collective-permute-done
  90.4 1.3 collective-permute-start.1
  92.2 3.9 %collective-permute-done.1 = bf16[3,128]{1,0:T(4,128)(2,1)S(1)} collective-permute-done((bf16[3,128]{1,0:T(4,128)(2,1)S(1)}, bf16[3,128]{1,0:T(4,128)(2,1)S(1)}, u32[]{:S(2)}, u32[]{:S(2)}) %collective-permute-start.1) | collective-permute-done | bytes 800 | tf_op jit(solution)/shard_map/ppermute | solution.py:12
  96.1 0.7 fusion
  96.9 2.0 %pad_maximum_fusion = bf16[3,4096,128]{1,2,0:T(8,128)(2,1)} fusion(bf16[1,4096,128]{1,2,0:T(8,128)(2,1)S(1)} %fusion.2, bf16[2,4096,128]{1,2,0:T(8,128)(2,1)S(1)} %fusion), kind=kLoop, calls=%fused_computation.6 | loop fusion | flops 1572864 | bytes 6291456 | tf_op jit(solution)/shard_map/concatenate | solution.py:101
  98.9 1.1 slice-done
  100.5 2.3 %fusion.1 = bf16[4096,128]{1,0:T(8,128)(2,1)S(1)} fusion(bf16[3,4096,128]{2,1,0:T(8,128)(2,1)} %all-gather.2.cloned.1.call-done, bf16[128,1,128]{2,0,1:T(8,128)(2,1)S(1)} %fusion.34, bf16[128,1,128]{2,0,1:T(8,128)(2,1)S(1)} %fusion.35), kind=kOutput, calls=%fused_computation.3 | convolution fusion | flops 269090816 | bytes 4259840 | tf_op jit(solution)/shard_map/tpe,pde->dt/dot_general | solution.py:95
  103.2 5.4 %all_to_all.46 = bf16[32,2,64,2,128]{4,2,0,3,1:T(8,128)(2,1)S(1)} all-to-all(bf16[32,2,64,2,128]{4,2,0,3,1:T(8,128)(2,1)S(1)} %copy.66), channel_id=1, replica_groups=mesh['chip'=32,'core'=2,'seq'=8] {'core'}, dimensions={1} | all-to-all | bytes 4194304 | tf_op jit(solution)/shard_map/all_to_all | solution.py:36
  108.7 0.6 broadcast_in_dim.24
  109.3 6.5 %all-to-all-start.4 = ((bf16[8,15,128]{2,1,0:T(8,128)(2,1)}), bf16[8,15,128]{2,1,0:T(8,128)(2,1)S(1)}, u32[]{:S(2)}, u32[]{:S(2)}) async-start(bf16[8,15,128]{2,1,0:T(8,128)(2,1)} %broadcast_in_dim.24), calls=%async_computation.5 | async-start | bytes 65536 | tf_op jit(solution)/shard_map/all_to_all | solution.py:107
  115.8 0.6 reduce_sum.75
  116.4 1.1 copy.68
  117.5 4.6 %all-to-all-done.4 = bf16[8,15,128]{2,1,0:T(8,128)(2,1)S(1)} async-done(((bf16[8,15,128]{2,1,0:T(8,128)(2,1)}), bf16[8,15,128]{2,1,0:T(8,128)(2,1)S(1)}, u32[]{:S(2)}, u32[]{:S(2)}) %all-to-all-start.4) | async-done | bytes 30752 | tf_op jit(solution)/shard_map/all_to_all | solution.py:107
  122.1 12.3 %all-to-all-start.3 = ((bf16[32,64,2,128]{3,1,2,0:T(8,128)(2,1)}), bf16[32,64,2,128]{3,1,2,0:T(8,128)(2,1)S(1)}, u32[]{:S(2)}, u32[]{:S(2)}) async-start(bf16[32,64,2,128]{3,1,2,0:T(8,128)(2,1)} %copy.68), calls=%async_computation.3 | async-start | bytes 2097152 | tf_op jit(solution)/shard_map/all_to_all | solution.py:38
  134.4 0.6 slice.120
  135.5 36.3 %all-to-all-done.3 = bf16[32,64,2,128]{3,1,2,0:T(8,128)(2,1)S(1)} async-done(((bf16[32,64,2,128]{3,1,2,0:T(8,128)(2,1)}), bf16[32,64,2,128]{3,1,2,0:T(8,128)(2,1)S(1)}, u32[]{:S(2)}, u32[]{:S(2)}) %all-to-all-start.3) | async-done | bytes 1048608 | tf_op jit(solution)/shard_map/all_to_all | solution.py:38
  172.0 0.6 slice_bitcast_fusion.9
  172.6 2.4 %reduce-scatter.2.cloned.1.call-done = bf16[3,512,128]{1,2,0:T(8,128)(2,1)} async-done(((bf16[3,4096,128]{1,2,0:T(8,128)(2,1)}), bf16[3,512,128]{1,2,0:T(8,128)(2,1)}) %reduce-scatter.2.cloned.1.call-update) | async-done | bytes 393232 | tf_op jit(solution)/shard_map/reduce_scatter | solution.py:102
  175.0 1.1 slice.140
  176.1 1.0 copy.72
  177.2 0.7 slice_bitcast_fusion.6
  (35 shorter events, 3.2 us)
Async XLA Ops:
  7.2 76.6 %all-gather.2.cloned.1.call-start = ((), (), s32[]{:S(2)}) async-start(), calls=%async_computation.6 | async-start | bytes 3538944 | tf_op jit(solution)/shard_map/all_gather | solution.py:47
  8.2 19.9 %copy-start.3 = (bf16[128]{0:T(256)(128)(2,1)S(1)}, bf16[128]{0:T(256)(128)(2,1)}, u32[]{:S(2)}) copy-start(bf16[128]{0:T(256)(128)(2,1)} %param.9) | copy-start | bytes 772
  8.2 19.9 %copy-start.2 = (bf16[4,128]{1,0:T(4,128)(2,1)S(1)}, bf16[4,128]{1,0:T(4,128)(2,1)}, u32[]{:S(2)}) copy-start(bf16[4,128]{1,0:T(4,128)(2,1)} %param.8) | copy-start | bytes 3076
  12.0 53.1 %all-to-all-start = ((bf16[32,128,2,64]{1,3,2,0:T(8,128)(2,1)}), bf16[32,128,2,64]{1,3,2,0:T(8,128)(2,1)S(1)}, u32[]{:S(2)}, u32[]{:S(2)}) async-start(bf16[32,128,2,64]{1,3,2,0:T(8,128)(2,1)} %broadcast_in_dim.19), calls=%async_computation | async-start | bytes 2097152 | tf_op jit(solution)/shard_map/all_to_all | solution.py:22
  28.1 146.9 %reduce-scatter.2.cloned.1.call-start = ((), (), s32[]{:S(2)}) async-start(), calls=%async_computation.7 | async-start | bytes 3538944 | tf_op jit(solution)/shard_map/reduce_scatter | solution.py:102
  83.8 6.0 %copy-start = (bf16[3,4096,128]{2,1,0:T(8,128)(2,1)S(1)}, bf16[3,4096,128]{2,1,0:T(8,128)(2,1)}, u32[]{:S(2)}) copy-start(bf16[3,4096,128]{2,1,0:T(8,128)(2,1)} %all-gather.2.cloned.1.call-done) | copy-start | bytes 9437188
  86.2 3.7 %collective-permute-start = (bf16[3,128]{1,0:T(4,128)(2,1)S(1)}, bf16[3,128]{1,0:T(4,128)(2,1)S(1)}, u32[]{:S(2)}, u32[]{:S(2)}) collective-permute-start(bf16[3,128]{1,0:T(4,128)(2,1)S(1)} %slice_bitcast_fusion.11), channel_id=1, source_target_pairs={{0,1},{1,2},{2,3},{3,4},{4,5},{5,6},{6,7},{8,9},{9,10},{10,11},{11... | collective-permute-start | bytes 2312 | tf_op jit(solution)/shard_map/ppermute | solution.py:12
  90.4 5.7 %collective-permute-start.1 = (bf16[3,128]{1,0:T(4,128)(2,1)S(1)}, bf16[3,128]{1,0:T(4,128)(2,1)S(1)}, u32[]{:S(2)}, u32[]{:S(2)}) collective-permute-start(bf16[3,128]{1,0:T(4,128)(2,1)S(1)} %slice.133), channel_id=1, source_target_pairs={{1,0},{2,1},{3,2},{4,3},{5,4},{6,5},{7,6},{9,8},{10,9},{11,10},{12... | collective-permute-start | bytes 2312 | tf_op jit(solution)/shard_map/ppermute | solution.py:12
  98.8 1.2 slice-start
  109.3 12.9 %all-to-all-start.4 = ((bf16[8,15,128]{2,1,0:T(8,128)(2,1)}), bf16[8,15,128]{2,1,0:T(8,128)(2,1)S(1)}, u32[]{:S(2)}, u32[]{:S(2)}) async-start(bf16[8,15,128]{2,1,0:T(8,128)(2,1)} %broadcast_in_dim.24), calls=%async_computation.5 | async-start | bytes 65536 | tf_op jit(solution)/shard_map/all_to_all | solution.py:107
  122.1 49.7 %all-to-all-start.3 = ((bf16[32,64,2,128]{3,1,2,0:T(8,128)(2,1)}), bf16[32,64,2,128]{3,1,2,0:T(8,128)(2,1)S(1)}, u32[]{:S(2)}, u32[]{:S(2)}) async-start(bf16[32,64,2,128]{3,1,2,0:T(8,128)(2,1)} %copy.68), calls=%async_computation.3 | async-start | bytes 2097152 | tf_op jit(solution)/shard_map/all_to_all | solution.py:38
  175.0 2.1 %copy-start.1 = (bf16[3,512,128]{1,2,0:T(8,128)(2,1)S(1)}, bf16[3,512,128]{1,2,0:T(8,128)(2,1)}, u32[]{:S(2)}) copy-start(bf16[3,512,128]{1,2,0:T(8,128)(2,1)} %reduce-scatter.2.cloned.1.call-done) | copy-start | bytes 1179652
Sparse Core Ops, SparseCore 0:
  10.7 73.1 all-gather.1
  99.0 75.9 reduce-scatter.1
where the time goes:
time: 185 us
  waiting for transfers between devices  97.8 us (53%)
  starting transfers between devices  38.6 us (21%)
  between operations  14.3 us (8%)
  local copies, waits for them, and re-layouts  10.8 us (6%)
  blocking collectives  10.8 us (6%)
  matrix products  6.81 us (4%)
  other arithmetic  5.69 us (3%)
    all_to_all x1, waiting for transfers between devices, gather_over(): return lax.all_to_all(rep, axis, 0, dim + 1, tiled=True)[0]  37 us
    all_to_all x1, waiting for transfers between devices, reduce_over_dp(): lax.all_to_all(split, 'chip', 0, 0, tiled=True).astype(jnp.float32)  36.3 us
    all_to_all x1, starting transfers between devices, gather_over(): return lax.all_to_all(rep, axis, 0, dim + 1, tiled=True)[0]  16.1 us
    all_gather x1, waiting for transfers between devices, on_device(): w_full = lax.all_gather(w_local, 'seq', axis=1, tiled=True)  12.4 us
    all_to_all x1, starting transfers between devices, reduce_over_dp(): lax.all_to_all(split, 'chip', 0, 0, tiled=True).astype(jnp.float32)  12.3 us
    all_to_all x1, starting transfers between devices, on_device(): lax.all_to_all(conv_parts, 'seq', 0, 0, tiled=True).astype(jnp.float32)  6.5 us
    all_to_all x1, blocking collectives, gather_over(): return lax.all_to_all(rep, axis, 0, dim + 1, tiled=True)[0]  5.42 us
    all_to_all x1, blocking collectives, reduce_over_dp(): lax.all_to_all(split, 'core', 1, 1, tiled=True).astype(jnp.float32)  5.42 us
  transfers between devices with their start and end apart: 7, of which 7 were waited for; matrix products, arithmetic and copies ran while one was open for 6% of the time, Pallas kernels for 0%

commit v1 on v0

--- a/solution.py
+++ b/solution.py
@@ -44,7 +44,9 @@
     n_core = lax.axis_size("core")
     n_dp = n_chip * n_core
     w_local = jnp.concatenate([in_weight, out_weight.T[None]], axis=0)
-    w_full = lax.all_gather(w_local, "seq", axis=1, tiled=True)
+    w_full = jnp.concatenate(
+        lax.all_to_all(jnp.stack([w_local] * lax.axis_size("seq")), "seq", 0, 0), axis=1
+    )
     in_full = w_full[:2]
     out_full_t = w_full[2]
     acts = gather_over(jnp.stack([tokens, grad_out], axis=1), "chip", n_chip, 2)

time: 185 us -> 207 us (1.12)
  the two profiles are of different devices: /device:TPU:16 before, /device:TPU:40 now
where the time goes in v1:
time: 207 us; the launch traced here: 206 us
  waiting for transfers between devices  112 us (54%)
  starting transfers between devices  42.5 us (21%)
  local copies, waits for them, and re-layouts  18.1 us (9%)
  between operations  14.3 us (7%)
  blocking collectives  11.7 us (6%)
  other arithmetic  3.99 us (2%)
  matrix products  3.48 us (2%)
    all_to_all x1, waiting for transfers between devices, reduce_over_dp(): lax.all_to_all(split, 'chip', 0, 0, tiled=True).astype(jnp.float32)  35 us
    all_to_all x1, waiting for transfers between devices, on_device(): lax.all_to_all(jnp.stack([w_local] * lax.axis_size('seq')), 'seq', 0, 0)  33.8 us
    all_to_all x1, waiting for transfers between devices, gather_over(): return lax.all_to_all(rep, axis, 0, dim + 1, tiled=True)[0]  27.4 us
    all_to_all x1, starting transfers between devices, gather_over(): return lax.all_to_all(rep, axis, 0, dim + 1, tiled=True)[0]  15.8 us
    all_to_all x1, starting transfers between devices, reduce_over_dp(): lax.all_to_all(split, 'chip', 0, 0, tiled=True).astype(jnp.float32)  9.25 us
    all_to_all x1, starting transfers between devices, on_device(): lax.all_to_all(jnp.stack([w_local] * lax.axis_size('seq')), 'seq', 0, 0)  8.79 us
    ppermute x2, waiting for transfers between devices, from_behind(): return lax.ppermute(block, axis, route)  7.66 us
    all_to_all x1, blocking collectives, gather_over(): return lax.all_to_all(rep, axis, 0, dim + 1, tiled=True)[0]  6.31 us
  transfers between devices with their start and end apart: 7, of which 7 were waited for; matrix products, arithmetic and copies ran while one was open for 5% of the time, Pallas kernels for 0%

profile of v1, /device:TPU:40, one launch (start us, length us, event | category | flops | bytes accessed | tf_op | source)
XLA Modules:
  0.0 205.9 jit_solution(4717775127092235895)
XLA Ops:
  7.2 0.8 pad_maximum_fusion.8
  8.0 1.2 broadcast_in_dim.19
  9.2 15.8 %all-to-all-start.1 = ((bf16[32,128,2,64]{1,3,2,0:T(8,128)(2,1)}), bf16[32,128,2,64]{1,3,2,0:T(8,128)(2,1)S(1)}, u32[]{:S(2)}, u32[]{:S(2)}) async-start(bf16[32,128,2,64]{1,3,2,0:T(8,128)(2,1)} %broadcast_in_dim.19), calls=%async_computation.1 | async-start | bytes 2097152 | tf_op jit(solution)/shard_map/all_to_all | solution.py:22
  25.3 27.4 %all-to-all-done.1 = bf16[32,128,2,64]{1,3,2,0:T(8,128)(2,1)S(1)} async-done(((bf16[32,128,2,64]{1,3,2,0:T(8,128)(2,1)}), bf16[32,128,2,64]{1,3,2,0:T(8,128)(2,1)S(1)}, u32[]{:S(2)}, u32[]{:S(2)}) %all-to-all-start.1) | async-done | bytes 1048608 | tf_op jit(solution)/shard_map/all_to_all | solution.py:22
  52.7 0.6 broadcast_in_dim.21
  53.4 6.3 %all_to_all.50 = bf16[2,128,2,32,1,64]{1,5,3,2,4,0:T(8,128)(2,1)} all-to-all(bf16[2,128,2,32,1,64]{1,5,3,2,4,0:T(8,128)(2,1)S(1)} %broadcast_in_dim.21), channel_id=1, replica_groups=mesh['chip'=32,'core'=2,'seq'=8] {'core'}, dimensions={0} | all-to-all | bytes 4194304 | tf_op jit(solution)/shard_map/all_to_all | solution.py:22
  59.7 2.3 %stack.46 = bf16[8,3,512,128]{3,2,1,0:T(8,128)(2,1)} broadcast(bf16[3,512,128]{2,1,0:T(8,128)(2,1)S(1)} %pad_maximum_fusion.2), dimensions={1,2,3} | broadcast | bytes 3538944 | tf_op jit(solution)/shard_map/stack | solution.py:48
  62.0 8.8 %all-to-all-start = ((bf16[8,3,512,128]{3,2,1,0:T(8,128)(2,1)}), bf16[8,3,512,128]{3,2,1,0:T(8,128)(2,1)S(1)}, u32[]{:S(2)}, u32[]{:S(2)}) async-start(bf16[8,3,512,128]{3,2,1,0:T(8,128)(2,1)} %stack.46), calls=%async_computation | async-start | bytes 6291456 | tf_op jit(solution)/shard_map/all_to_all | solution.py:48
  70.8 3.2 %copy.74 = bf16[2,128,2,32,1,64]{1,5,0,3,2,4:T(8,128)(2,1)} copy(bf16[2,128,2,32,1,64]{1,5,3,2,4,0:T(8,128)(2,1)} %all_to_all.50) | data formatting | bytes 4194304 | tf_op jit(solution)/shard_map/all_to_all | solution.py:22
  74.0 33.8 %all-to-all-done = bf16[8,3,512,128]{3,2,1,0:T(8,128)(2,1)S(1)} async-done(((bf16[8,3,512,128]{3,2,1,0:T(8,128)(2,1)}), bf16[8,3,512,128]{3,2,1,0:T(8,128)(2,1)S(1)}, u32[]{:S(2)}, u32[]{:S(2)}) %all-to-all-start) | async-done | bytes 3145760 | tf_op jit(solution)/shard_map/all_to_all | solution.py:48
  108.2 2.1 %copy-done = bf16[2,128,2,32,1,64]{1,5,0,3,2,4:T(8,128)(2,1)S(1)} copy-done((bf16[2,128,2,32,1,64]{1,5,0,3,2,4:T(8,128)(2,1)S(1)}, bf16[2,128,2,32,1,64]{1,5,0,3,2,4:T(8,128)(2,1)}, u32[]{:S(2)}) %copy-start) | copy-done | bytes 2097176
  110.9 2.8 %collective-permute-start = (bf16[3,128]{1,0:T(4,128)(2,1)S(1)}, bf16[3,128]{1,0:T(4,128)(2,1)S(1)}, u32[]{:S(2)}, u32[]{:S(2)}) collective-permute-start(bf16[3,128]{1,0:T(4,128)(2,1)S(1)} %slice_bitcast_fusion.11), channel_id=1, source_target_pairs={{0,1},{1,2},{2,3},{3,4},{4,5},{5,6},{6,7},{8,9},{9,10},{10,11},{11... | collective-permute-start | bytes 2312 | tf_op jit(solution)/shard_map/ppermute | solution.py:12
  113.8 4.7 %collective-permute-done = bf16[3,128]{1,0:T(4,128)(2,1)S(1)} collective-permute-done((bf16[3,128]{1,0:T(4,128)(2,1)S(1)}, bf16[3,128]{1,0:T(4,128)(2,1)S(1)}, u32[]{:S(2)}, u32[]{:S(2)}) %collective-permute-start) | collective-permute-done | bytes 800 | tf_op jit(solution)/shard_map/ppermute | solution.py:12
  119.0 1.9 collective-permute-start.1
  121.5 3.0 %collective-permute-done.1 = bf16[3,128]{1,0:T(4,128)(2,1)S(1)} collective-permute-done((bf16[3,128]{1,0:T(4,128)(2,1)S(1)}, bf16[3,128]{1,0:T(4,128)(2,1)S(1)}, u32[]{:S(2)}, u32[]{:S(2)}) %collective-permute-start.1) | collective-permute-done | bytes 800 | tf_op jit(solution)/shard_map/ppermute | solution.py:12
  124.5 0.7 fusion
  125.3 1.9 pad_maximum_fusion
  127.3 1.1 copy-done.2
  129.1 0.7 fusion.4
  130.4 5.4 %all_to_all.51 = bf16[32,2,64,2,128]{4,2,0,3,1:T(8,128)(2,1)S(1)} all-to-all(bf16[32,2,64,2,128]{4,2,0,3,1:T(8,128)(2,1)S(1)} %copy.79), channel_id=1, replica_groups=mesh['chip'=32,'core'=2,'seq'=8] {'core'}, dimensions={1} | all-to-all | bytes 4194304 | tf_op jit(solution)/shard_map/all_to_all | solution.py:36
  135.8 0.6 broadcast_in_dim.24
  136.4 4.0 %all-to-all-start.5 = ((bf16[8,15,128]{2,1,0:T(8,128)(2,1)}), bf16[8,15,128]{2,1,0:T(8,128)(2,1)S(1)}, u32[]{:S(2)}, u32[]{:S(2)}) async-start(bf16[8,15,128]{2,1,0:T(8,128)(2,1)} %broadcast_in_dim.24), calls=%async_computation.6 | async-start | bytes 65536 | tf_op jit(solution)/shard_map/all_to_all | solution.py:109
  140.4 0.6 reduce_sum.75
  141.0 1.1 copy.81
  142.1 3.2 %all-to-all-done.5 = bf16[8,15,128]{2,1,0:T(8,128)(2,1)S(1)} async-done(((bf16[8,15,128]{2,1,0:T(8,128)(2,1)}), bf16[8,15,128]{2,1,0:T(8,128)(2,1)S(1)}, u32[]{:S(2)}, u32[]{:S(2)}) %all-to-all-start.5) | async-done | bytes 30752 | tf_op jit(solution)/shard_map/all_to_all | solution.py:109
  145.3 9.2 %all-to-all-start.4 = ((bf16[32,64,2,128]{3,1,2,0:T(8,128)(2,1)}), bf16[32,64,2,128]{3,1,2,0:T(8,128)(2,1)S(1)}, u32[]{:S(2)}, u32[]{:S(2)}) async-start(bf16[32,64,2,128]{3,1,2,0:T(8,128)(2,1)} %copy.81), calls=%async_computation.4 | async-start | bytes 2097152 | tf_op jit(solution)/shard_map/all_to_all | solution.py:38
  155.7 35.0 %all-to-all-done.4 = bf16[32,64,2,128]{3,1,2,0:T(8,128)(2,1)S(1)} async-done(((bf16[32,64,2,128]{3,1,2,0:T(8,128)(2,1)}), bf16[32,64,2,128]{3,1,2,0:T(8,128)(2,1)S(1)}, u32[]{:S(2)}, u32[]{:S(2)}) %all-to-all-start.4) | async-done | bytes 1048608 | tf_op jit(solution)/shard_map/all_to_all | solution.py:38
  190.8 0.6 slice_bitcast_fusion.9
  191.4 4.7 %reduce-scatter.2.cloned.1.call-done = bf16[3,512,128]{1,2,0:T(8,128)(2,1)} async-done(((bf16[3,4096,128]{1,2,0:T(8,128)(2,1)}), bf16[3,512,128]{1,2,0:T(8,128)(2,1)}) %reduce-scatter.2.cloned.1.call-update) | async-done | bytes 393232 | tf_op jit(solution)/shard_map/reduce_scatter | solution.py:104
  196.1 1.1 slice.145
  197.2 1.0 copy.85
  198.3 0.7 slice_bitcast_fusion.6
  (49 shorter events, 5.0 us)
Async XLA Ops:
  7.2 17.9 %copy-start.7 = (bf16[128,512]{1,0:T(8,128)(2,1)S(1)}, bf16[128,512]{1,0:T(8,128)(2,1)}, u32[]{:S(2)}) copy-start(bf16[128,512]{1,0:T(8,128)(2,1)} %param.10) | copy-start | bytes 393220
  7.2 18.0 %copy-start.6 = (bf16[2,512,128]{2,1,0:T(8,128)(2,1)S(1)}, bf16[2,512,128]{2,1,0:T(8,128)(2,1)}, u32[]{:S(2)}) copy-start(bf16[2,512,128]{2,1,0:T(8,128)(2,1)} %param.7) | copy-start | bytes 786436
  9.2 43.4 %all-to-all-start.1 = ((bf16[32,128,2,64]{1,3,2,0:T(8,128)(2,1)}), bf16[32,128,2,64]{1,3,2,0:T(8,128)(2,1)S(1)}, u32[]{:S(2)}, u32[]{:S(2)}) async-start(bf16[32,128,2,64]{1,3,2,0:T(8,128)(2,1)} %broadcast_in_dim.19), calls=%async_computation.1 | async-start | bytes 2097152 | tf_op jit(solution)/shard_map/all_to_all | solution.py:22
  62.0 8.8 %copy-start.9 = (bf16[128]{0:T(256)(128)(2,1)S(1)}, bf16[128]{0:T(256)(128)(2,1)}, u32[]{:S(2)}) copy-start(bf16[128]{0:T(256)(128)(2,1)} %param.9) | copy-start | bytes 772
  62.0 8.8 %copy-start.8 = (bf16[4,128]{1,0:T(4,128)(2,1)S(1)}, bf16[4,128]{1,0:T(4,128)(2,1)}, u32[]{:S(2)}) copy-start(bf16[4,128]{1,0:T(4,128)(2,1)} %param.8) | copy-start | bytes 3076
  62.0 45.8 %all-to-all-start = ((bf16[8,3,512,128]{3,2,1,0:T(8,128)(2,1)}), bf16[8,3,512,128]{3,2,1,0:T(8,128)(2,1)S(1)}, u32[]{:S(2)}, u32[]{:S(2)}) async-start(bf16[8,3,512,128]{3,2,1,0:T(8,128)(2,1)} %stack.46), calls=%async_computation | async-start | bytes 6291456 | tf_op jit(solution)/shard_map/all_to_all | solution.py:48
  70.8 125.3 %reduce-scatter.2.cloned.1.call-start = ((), (), s32[]{:S(2)}) async-start(), calls=%async_computation.7 | async-start | bytes 3538944 | tf_op jit(solution)/shard_map/reduce_scatter | solution.py:104
  108.0 2.3 %copy-start = (bf16[2,128,2,32,1,64]{1,5,0,3,2,4:T(8,128)(2,1)S(1)}, bf16[2,128,2,32,1,64]{1,5,0,3,2,4:T(8,128)(2,1)}, u32[]{:S(2)}) copy-start(bf16[2,128,2,32,1,64]{1,5,0,3,2,4:T(8,128)(2,1)} %copy.74) | copy-start | bytes 6291460
  108.2 5.6 %copy-start.4 = (bf16[2,8,512,128]{3,2,1,0:T(8,128)(2,1)}, bf16[2,8,512,128]{3,2,1,0:T(8,128)(2,1)S(1)}, u32[]{:S(2)}) copy-start(bf16[2,8,512,128]{3,2,1,0:T(8,128)(2,1)S(1)} %copy.76) | copy-start | bytes 6291460
  110.9 7.6 %collective-permute-start = (bf16[3,128]{1,0:T(4,128)(2,1)S(1)}, bf16[3,128]{1,0:T(4,128)(2,1)S(1)}, u32[]{:S(2)}, u32[]{:S(2)}) collective-permute-start(bf16[3,128]{1,0:T(4,128)(2,1)S(1)} %slice_bitcast_fusion.11), channel_id=1, source_target_pairs={{0,1},{1,2},{2,3},{3,4},{4,5},{5,6},{6,7},{8,9},{9,10},{10,11},{11... | collective-permute-start | bytes 2312 | tf_op jit(solution)/shard_map/ppermute | solution.py:12
  113.8 4.7 %copy-start.1 = (bf16[1,8,512,128]{3,2,0,1:T(8,128)(2,1)}, bf16[1,8,512,128]{3,2,0,1:T(8,128)(2,1)S(1)}, u32[]{:S(2)}) copy-start(bf16[1,8,512,128]{3,2,0,1:T(8,128)(2,1)S(1)} %slice.127) | copy-start | bytes 3145732
  119.0 5.5 %collective-permute-start.1 = (bf16[3,128]{1,0:T(4,128)(2,1)S(1)}, bf16[3,128]{1,0:T(4,128)(2,1)S(1)}, u32[]{:S(2)}, u32[]{:S(2)}) collective-permute-start(bf16[3,128]{1,0:T(4,128)(2,1)S(1)} %slice.138), channel_id=1, source_target_pairs={{1,0},{2,1},{3,2},{4,3},{5,4},{6,5},{7,6},{9,8},{10,9},{11,10},{12... | collective-permute-start | bytes 2312 | tf_op jit(solution)/shard_map/ppermute | solution.py:12
  127.2 1.2 copy-start.2
  127.2 1.9 copy-start.5
  136.4 8.9 %all-to-all-start.5 = ((bf16[8,15,128]{2,1,0:T(8,128)(2,1)}), bf16[8,15,128]{2,1,0:T(8,128)(2,1)S(1)}, u32[]{:S(2)}, u32[]{:S(2)}) async-start(bf16[8,15,128]{2,1,0:T(8,128)(2,1)} %broadcast_in_dim.24), calls=%async_computation.6 | async-start | bytes 65536 | tf_op jit(solution)/shard_map/all_to_all | solution.py:109
  145.3 45.4 %all-to-all-start.4 = ((bf16[32,64,2,128]{3,1,2,0:T(8,128)(2,1)}), bf16[32,64,2,128]{3,1,2,0:T(8,128)(2,1)S(1)}, u32[]{:S(2)}, u32[]{:S(2)}) async-start(bf16[32,64,2,128]{3,1,2,0:T(8,128)(2,1)} %copy.81), calls=%async_computation.4 | async-start | bytes 2097152 | tf_op jit(solution)/shard_map/all_to_all | solution.py:38
  196.1 2.1 %copy-start.3 = (bf16[3,512,128]{1,2,0:T(8,128)(2,1)S(1)}, bf16[3,512,128]{1,2,0:T(8,128)(2,1)}, u32[]{:S(2)}) copy-start(bf16[3,512,128]{1,2,0:T(8,128)(2,1)} %reduce-scatter.2.cloned.1.call-done) | copy-start | bytes 1179652
Sparse Core Ops, SparseCore 0:
  127.4 68.7 reduce-scatter.1
